TPU v7x, 32 devices: a whole 2x2x4 slice. The times are simulated.
32 devices in a mesh: outer: 4 (over z), dp: 2 (over y), cent: 4 (over x, core).
Axes of the slice: x: 2, y: 2, z: 4, core: 2. Of those that a mesh axis runs over, the one named last changes fastest.
Arguments:
- rows: float32 [2048, 1024], P(('outer', 'dp')), may hold values from -256 to 256
- centroids: float32 [4096, 1024], P(('dp', 'cent')), may hold values from -0.5 to 0.5
Outputs:
- centroid_shift: float32 [4096, 1024], P(('dp', 'cent'))
All inputs are finite; a program needn't handle non-finite values.
Results may differ from a plain program's by a relative error of at most 0.0081.
Values may be sent and summed in bfloat16 or wider, within the bound.
No kernel may reach another device: no remote copies, remote signals or barrier semaphores. Data moves between devices by JAX's collectives and lax.ppermute only.
A program may use at most 64 MiB of HBM per device.

v0:
```python
import jax
import jax.numpy as jnp
from jax import lax
from jax.sharding import PartitionSpec as P


def scores_for(piece, cent_bf, squares):
    product = lax.dot_general(
        piece, cent_bf, (((1,), (1,)), ((), ())), preferred_element_type=jnp.float32
    )
    return 0.5 * (2.0 * product - squares[None, :])


def row_summary(logits):
    local_max = jnp.max(logits, axis=1)
    local_sum = jnp.sum(jnp.exp(logits - local_max[:, None]), axis=1)
    return (local_max, local_sum)


def global_stats(local_max, local_sum):
    row_peak = lax.pmax(local_max, ("dp", "cent"))
    row_mass = lax.psum(local_sum * jnp.exp(local_max - row_peak), ("dp", "cent"))
    return (row_peak, row_mass)


def shards(rows, centroids):
    rows_bf = rows.astype(jnp.bfloat16)
    cent_bf = centroids.astype(jnp.bfloat16)
    squares = jnp.sum(centroids * centroids, axis=1)
    gathered = lax.all_gather(rows_bf, "dp", axis=0, tiled=True)
    logits = scores_for(gathered, cent_bf, squares)
    local_max, local_sum = row_summary(logits)
    row_peak, row_mass = global_stats(local_max, local_sum)
    weights = (jnp.exp(logits - row_peak[:, None]) / row_mass[:, None]).astype(jnp.bfloat16)
    weight_sum = jnp.sum(weights.astype(jnp.float32), axis=0)
    pull = lax.dot_general(
        weights, gathered, (((0,), (0,)), ((), ())), preferred_element_type=jnp.float32
    )
    delta = (pull - weight_sum[:, None] * centroids) / (weight_sum[:, None] + 1.0)
    return lax.psum(delta, "outer") / lax.axis_size("outer")


def solution(mesh):
    return jax.shard_map(
        shards,
        mesh=mesh,
        in_specs=(P(("outer", "dp"), None), P(("dp", "cent"), None)),
        out_specs=P(("dp", "cent"), None),
        check_vma=False,
    )
```

profile of v0, /device:TPU:0, one launch (start us, length us, event | category | flops | bytes accessed | tf_op | source)
XLA Modules:
  0.0 160.0 jit_solution(11891567191275131057)
XLA Ops:
  6.5 0.0 copy-start
  6.5 0.0 all-gather.2.cloned.1.call-start
  6.5 2.2 %convert_element_type.12 = bf16[256,1024]{1,0:T(8,128)(2,1)} convert(f32[256,1024]{1,0:T(8,128)} %param.2) | non-fusion elementwise | flops 262144 | bytes 1572864 | tf_op jit(solution)/shard_map/convert_element_type | solution.py:27
  8.8 0.0 all-gather.2.cloned.1.call-update
  8.8 0.0 all-reduce.2.cloned.1.call-start
  8.9 0.0 copy-done
  8.9 0.2 multiply_reduce_fusion
  9.1 23.9 %all-gather.2.cloned.1.call-done = bf16[512,1024]{1,0:T(8,128)(2,1)} async-done(((bf16[256,1024]{1,0:T(8,128)(2,1)}), bf16[512,1024]{1,0:T(8,128)(2,1)}) %all-gather.2.cloned.1.call-update) | async-done | bytes 1048592 | tf_op jit(solution)/shard_map/all_gather | solution.py:30
  33.0 2.0 %fusion.3 = (f32[512]{0:T(512)S(1)}, f32[512,512]{0,1:T(8,128)S(1)}) fusion(f32[512]{0:T(512)S(1)} %multiply_reduce_fusion, bf16[512,1024]{1,0:T(8,128)(2,1)} %all-gather.2.cloned.1.call-done, f32[512,1024]{1,0:T(8,128)S(1)} %copy-done), kind=kOutput, calls=%fused_computation.12 | convolution fusion | flops 538443264 | bytes 4198400 | tf_op jit(solution)/shard_map/dot_general | solution.py:8
  35.0 12.7 %pmax.7 = f32[512]{0:T(512)S(1)} all-reduce(f32[512]{0:T(512)S(1)} %get-tuple-element.7), channel_id=1, replica_groups=mesh['outer'=4,'dp'=2,'cent'=4] {'dp','cent'}, use_global_device_ids=true, to_apply=%region_2.0 | all-reduce | flops 512 | bytes 4096 | tf_op jit(solution)/shard_map/pmax | solution.py:21
  47.7 0.2 exponential_reduce_fusion
  47.9 11.8 %psum.14 = f32[512]{0:T(512)S(1)} all-reduce(f32[512]{0:T(512)S(1)} %exponential_multiply_fusion), channel_id=1, replica_groups=mesh['outer'=4,'dp'=2,'cent'=4] {'dp','cent'}, use_global_device_ids=true, to_apply=%region_4.0 | all-reduce | flops 512 | bytes 4096 | tf_op jit(solution)/shard_map/psum | solution.py:22
  59.7 0.3 convert_reduce_fusion
  60.0 3.3 %subtract_divide_fusion = f32[512,1024]{1,0:T(8,128)} fusion(f32[512,1024]{1,0:T(8,128)S(1)} %copy-done, bf16[512,512]{0,1:T(8,128)(2,1)S(1)} %get-tuple-element.6, bf16[512,1024]{1,0:T(8,128)(2,1)} %all-gather.2.cloned.1.call-done, f32[512]{0:T(512)S(1)} %broadcast_add_fusion, f32[512]{0:T(512)S(1)} %get-tuple-element.5), kind=kOutput, calls=%fused_computation | convolution fusion | flops 538443776 | bytes 5771264 | tf_op jit(solution)/shard_map/dot_general | solution.py:36
  63.3 0.0 all-reduce.2.cloned.1.call-update
  63.3 86.7 %all-reduce.2.cloned.1.call-done = f32[512,1024]{1,0:T(8,128)} async-done(((f32[512,1024]{1,0:T(8,128)}), f32[512,1024]{1,0:T(8,128)}) %all-reduce.2.cloned.1.call-update) | async-done | bytes 2097168 | tf_op jit(solution)/shard_map/psum | solution.py:40
  150.0 3.2 %broadcast_multiply_fusion = f32[512,1024]{1,0:T(8,128)} fusion(f32[512,1024]{1,0:T(8,128)} %all-reduce.2.cloned.1.call-done), kind=kLoop, calls=%fused_computation.5 | loop fusion | flops 524288 | bytes 4194304 | tf_op jit(solution)/shard_map/div | solution.py:40
  (2 shorter events, 0.0 us)
Async XLA Ops:
  6.5 2.3 %copy-start = (f32[512,1024]{1,0:T(8,128)S(1)}, f32[512,1024]{1,0:T(8,128)}, u32[]{:S(2)}) copy-start(f32[512,1024]{1,0:T(8,128)} %param.3) | copy-start | bytes 6291460
  6.5 26.4 %all-gather.2.cloned.1.call-start = ((), (), s32[]{:S(2)}) async-start(), calls=%async_computation | async-start | bytes 1572864 | tf_op jit(solution)/shard_map/all_gather | solution.py:30
  8.8 141.2 %all-reduce.2.cloned.1.call-start = ((), (), s32[]{:S(2)}) async-start(), calls=%async_computation.1 | async-start | bytes 4194304 | tf_op jit(solution)/shard_map/psum | solution.py:40
Sparse Core Ops, SparseCore 0:
  8.9 23.9 all-gather.1
  63.4 86.5 all-reduce.1
where the time goes:
time: 160 us
  waiting for transfers between devices  111 us (69%)
  blocking collectives  24.5 us (15%)
  between operations  13.4 us (8%)
  other arithmetic  6.15 us (4%)
  matrix products  5.29 us (3%)
    psum x1, waiting for transfers between devices, shards(): return lax.psum(delta, 'outer') / lax.axis_size('outer')  86.7 us
    all_gather x1, waiting for transfers between devices, shards(): gathered = lax.all_gather(rows_bf, 'dp', axis=0, tiled=True)  23.9 us
    pmax x1, blocking collectives, global_stats(): row_peak = lax.pmax(local_max, ('dp', 'cent'))  12.7 us
    psum x1, blocking collectives, global_stats(): lax.psum(local_sum * jnp.exp(local_max - row_peak), ('dp', 'cent'))  11.8 us
    dot_general x1, matrix products, shards(): lax.dot_general(weights, gathered, (((0,), (0,)), ((), ())), preferred_el...  3.3 us
    div x1, other arithmetic, shards(): return lax.psum(delta, 'outer') / lax.axis_size('outer')  3.22 us
  transfers between devices with their start and end apart: 2, of which 2 were waited for; matrix products, arithmetic and copies ran while one was open for 0% of the time, Pallas kernels for 0%

commit v1 on v0

--- a/solution.py
+++ b/solution.py
@@ -2,6 +2,23 @@
 import jax.numpy as jnp
 from jax import lax
 from jax.sharding import PartitionSpec as P
+
+
+def joined_along(blocks, dim):
+    blocks = jnp.moveaxis(blocks, 0, dim)
+    shape = blocks.shape
+    return blocks.reshape(*shape[:dim], shape[dim] * shape[dim + 1], *shape[dim + 2 :])
+
+
+def grow_blocks(x, axis):
+    size, index = (lax.axis_size(axis), lax.axis_index(axis))
+    parts, stride = (x[None], 1)
+    while stride < size:
+        other = lax.ppermute(parts, axis, [(i, i ^ stride) for i in range(size)])
+        low = index & stride == 0
+        parts = jnp.concatenate([jnp.where(low, parts, other), jnp.where(low, other, parts)])
+        stride *= 2
+    return parts
 
 
 def scores_for(piece, cent_bf, squares):
@@ -27,7 +44,7 @@
     rows_bf = rows.astype(jnp.bfloat16)
     cent_bf = centroids.astype(jnp.bfloat16)
     squares = jnp.sum(centroids * centroids, axis=1)
-    gathered = lax.all_gather(rows_bf, "dp", axis=0, tiled=True)
+    gathered = joined_along(grow_blocks(rows_bf, "dp"), 0)
     logits = scores_for(gathered, cent_bf, squares)
     local_max, local_sum = row_summary(logits)
     row_peak, row_mass = global_stats(local_max, local_sum)

time: 160 us -> 151 us (0.944)
  waiting for transfers between devices: 111 us -> 96.5 us
  starting transfers between devices: 0.04 us -> 2.97 us
  other arithmetic: 6.15 us -> 8.91 us
    all_gather x1 -> x0, waiting for transfers between devices: 23.9 us -> none  [shards(): gathered = lax.all_gather(rows_bf, 'dp', axis=0, tiled=True)]
    ppermute x0 -> x1, waiting for transfers between devices: none -> 10.4 us  [grow_blocks(): other = lax.ppermute(parts, axis, [(i, i ^ stride) for i in range(size)])]
    ppermute x0 -> x1, starting transfers between devices: none -> 2.97 us  [grow_blocks(): other = lax.ppermute(parts, axis, [(i, i ^ stride) for i in range(size)])]
    convert_element_type x1 -> x0, other arithmetic: 2.24 us -> none  [shards(): rows_bf = rows.astype(jnp.bfloat16)]
    broadcast_in_dim x0 -> x1, other arithmetic: none -> 2.18 us  [grow_blocks(): parts, stride = (x[None], 1)]
  transfers between devices with their start and end apart: 2 -> 2, of which waited for: 2 -> 2; matrix products, arithmetic and copies ran while one was open for 0% -> 1% of each run, Pallas kernels for 0% -> 0%
where the time goes in v1:
time: 151 us
  waiting for transfers between devices  96.5 us (64%)
  blocking collectives  24.8 us (16%)
  between operations  13.4 us (9%)
  other arithmetic  8.91 us (6%)
  matrix products  4.08 us (3%)
  starting transfers between devices  2.97 us (2%)
    psum x1, waiting for transfers between devices, shards(): return lax.psum(delta, 'outer') / lax.axis_size('outer')  86 us
    pmax x1, blocking collectives, global_stats(): row_peak = lax.pmax(local_max, ('dp', 'cent'))  13 us
    psum x1, blocking collectives, global_stats(): lax.psum(local_sum * jnp.exp(local_max - row_peak), ('dp', 'cent'))  11.8 us
    ppermute x1, waiting for transfers between devices, grow_blocks(): other = lax.ppermute(parts, axis, [(i, i ^ stride) for i in range(size)])  10.4 us
    dot_general x1, matrix products, shards(): lax.dot_general(weights, gathered, (((0,), (0,)), ((), ())), preferred_el...  3.3 us
    div x1, other arithmetic, shards(): return lax.psum(delta, 'outer') / lax.axis_size('outer')  3.22 us
  transfers between devices with their start and end apart: 2, of which 2 were waited for; matrix products, arithmetic and copies ran while one was open for 1% of the time, Pallas kernels for 0%

profile of v1, /device:TPU:0, one launch (start us, length us, event | category | flops | bytes accessed | tf_op | source)
XLA Modules:
  0.0 150.9 jit_solution(1358231808904108760)
XLA Ops:
  6.5 0.0 copy-start.2
  6.5 0.0 all-reduce.2.cloned.1.call-start
  6.5 2.2 %convert_bitcast_fusion = bf16[1,256,1024]{2,1,0:T(8,128)(2,1)} fusion(f32[256,1024]{1,0:T(8,128)} %param.2), kind=kLoop, calls=%fused_computation.11 | loop fusion | flops 262144 | bytes 1572864 | tf_op jit(solution)/shard_map/broadcast_in_dim | solution.py:15
  8.7 3.0 %collective-permute-start = (bf16[1,256,1024]{2,1,0:T(8,128)(2,1)}, bf16[1,256,1024]{2,1,0:T(8,128)(2,1)}, u32[]{:S(2)}, u32[]{:S(2)}) collective-permute-start(bf16[1,256,1024]{2,1,0:T(8,128)(2,1)} %convert_bitcast_fusion), channel_id=1, source_target_pairs={{0,4},{4,0},{1,5},{5,1},{2,6},{6,2},{3,7},{7,3},{8,12},{12,8},{9,1... | collective-permute-start | bytes 1572872 | tf_op jit(solution)/shard_map/ppermute | solution.py:17
  11.7 1.8 %multiply_reduce_fusion = f32[512]{0:T(512)S(1)} fusion(f32[512,1024]{1,0:T(8,128)} %param.3), kind=kLoop, calls=%fused_computation.1 | loop fusion | flops 1048064 | bytes 2099200 | tf_op jit(solution)/shard_map/reduce_sum | solution.py:46
  13.5 0.0 copy-start
  13.5 10.4 %collective-permute-done = bf16[1,256,1024]{2,1,0:T(8,128)(2,1)} collective-permute-done((bf16[1,256,1024]{2,1,0:T(8,128)(2,1)}, bf16[1,256,1024]{2,1,0:T(8,128)(2,1)}, u32[]{:S(2)}, u32[]{:S(2)}) %collective-permute-start) | collective-permute-done | bytes 524320 | tf_op jit(solution)/shard_map/ppermute | solution.py:17
  23.9 0.0 copy-done.2
  23.9 1.1 broadcast_select_fusion.1
  25.1 0.1 pad_maximum_fusion
  25.2 0.0 copy-start.1
  25.2 0.0 copy-done
  25.2 0.8 fusion.3
  26.0 0.2 copy-done.1
  26.2 13.0 %pmax.7 = f32[512]{0:T(512)S(1)} all-reduce(f32[512]{0:T(512)S(1)} %get-tuple-element.9), channel_id=1, replica_groups=mesh['outer'=4,'dp'=2,'cent'=4] {'dp','cent'}, use_global_device_ids=true, to_apply=%region_2.3 | all-reduce | flops 512 | bytes 4096 | tf_op jit(solution)/shard_map/pmax | solution.py:38
  39.2 0.2 exponential_reduce_fusion
  39.4 11.8 %psum.14 = f32[512]{0:T(512)S(1)} all-reduce(f32[512]{0:T(512)S(1)} %exponential_multiply_fusion), channel_id=1, replica_groups=mesh['outer'=4,'dp'=2,'cent'=4] {'dp','cent'}, use_global_device_ids=true, to_apply=%region_4.5 | all-reduce | flops 512 | bytes 4096 | tf_op jit(solution)/shard_map/psum | solution.py:39
  51.2 0.3 convert_reduce_fusion
  51.4 3.3 %subtract_divide_fusion = f32[512,1024]{1,0:T(8,128)} fusion(f32[512,1024]{1,0:T(8,128)S(1)} %copy-done, bf16[512,512]{0,1:T(8,128)(2,1)S(1)} %get-tuple-element.6, bf16[512,1024]{1,0:T(8,128)(2,1)} %bitcast.9, f32[512]{0:T(512)S(1)} %broadcast_add_fusion, f32[512]{0:T(512)S(1)} %get-tuple-element.5), kind=kOutput, calls=%fused_computation | convolution fusion | flops 538443776 | bytes 5771264 | tf_op jit(solution)/shard_map/dot_general | solution.py:53
  54.7 0.0 all-reduce.2.cloned.1.call-update
  54.8 86.0 %all-reduce.2.cloned.1.call-done = f32[512,1024]{1,0:T(8,128)} async-done(((f32[512,1024]{1,0:T(8,128)}), f32[512,1024]{1,0:T(8,128)}) %all-reduce.2.cloned.1.call-update) | async-done | bytes 2097168 | tf_op jit(solution)/shard_map/psum | solution.py:57
  140.8 3.2 %broadcast_multiply_fusion = f32[512,1024]{1,0:T(8,128)} fusion(f32[512,1024]{1,0:T(8,128)} %all-reduce.2.cloned.1.call-done), kind=kLoop, calls=%fused_computation.6 | loop fusion | flops 524288 | bytes 4194304 | tf_op jit(solution)/shard_map/div | solution.py:57
  (2 shorter events, 0.0 us)
Async XLA Ops:
  6.5 17.4 %copy-start.2 = (f32[256,1024]{1,0:T(8,128)S(1)}, f32[256,1024]{1,0:T(8,128)}, u32[]{:S(2)}) copy-start(f32[256,1024]{1,0:T(8,128)} %param.2) | copy-start | bytes 3145732
  6.5 134.3 %all-reduce.2.cloned.1.call-start = ((), (), s32[]{:S(2)}) async-start(), calls=%async_computation | async-start | bytes 4194304 | tf_op jit(solution)/shard_map/psum | solution.py:57
  8.7 15.2 %collective-permute-start = (bf16[1,256,1024]{2,1,0:T(8,128)(2,1)}, bf16[1,256,1024]{2,1,0:T(8,128)(2,1)}, u32[]{:S(2)}, u32[]{:S(2)}) collective-permute-start(bf16[1,256,1024]{2,1,0:T(8,128)(2,1)} %convert_bitcast_fusion), channel_id=1, source_target_pairs={{0,4},{4,0},{1,5},{5,1},{2,6},{6,2},{3,7},{7,3},{8,12},{12,8},{9,1... | collective-permute-start | bytes 1572872 | tf_op jit(solution)/shard_map/ppermute | solution.py:17
  13.5 11.7 %copy-start = (f32[512,1024]{1,0:T(8,128)S(1)}, f32[512,1024]{1,0:T(8,128)}, u32[]{:S(2)}) copy-start(f32[512,1024]{1,0:T(8,128)} %param.3) | copy-start | bytes 6291460
  25.2 1.0 copy-start.1
Sparse Core Ops, SparseCore 0:
  54.9 85.8 all-reduce.1
